TPU v7x, 32 devices: a whole 2x2x4 slice. The times are simulated.
32 devices in a mesh: exp: 4 (over z), row: 4 (over y, core), col: 2 (over x).
Axes of the slice: x: 2, y: 2, z: 4, core: 2. Of those that a mesh axis runs over, the one named last changes fastest.
Arguments:
- exposures: float32 [64, 128, 1024], P('exp', 'row', 'col'), may hold values from -6 to 6
- bad_pixels: int32 [64, 128, 1024], P('exp', 'row', 'col'), may hold values 0 or 1
- offsets: int32 [64, 2], P('exp'), may hold values from -8 to 8, as said below
- warp_index: int32 [64, 2], P('exp'), may hold values from 0 to 15
- blur_index: int32 [64], P('exp'), may hold values from 0 to 7
Outputs:
- residual: float32 [64, 128, 1024], P('exp', 'row', 'col')
- median_sky: float32 [128, 1024], P('row', 'col')
Inputs may be any that keep to these rules, and one draw needn't show every extreme that they name: `offsets`: in each component some exposure has the offset -8 and some has 8.
All inputs are finite; a program needn't handle non-finite values. No bound on the sum of `bad_pixels` on one device may be relied on, other than what follows from the above.
Results may differ from a plain program's by a relative error of at most 0.0003.
Values sent between devices are 32-bit elements; how exact they have to be, the bound alone decides.
No kernel may reach another device: no remote copies, remote signals or barrier semaphores. Data moves between devices by JAX's collectives and lax.ppermute only.
A program may use at most 64 MiB of HBM per device.

v0:
```python
import jax
import jax.numpy as jnp
from jax import lax
from jax.sharding import PartitionSpec as P

NFRAC = 16
NPSF = 8
PSF_RADIUS = 4
PASSES = 16
HALO = 11
sentinel = 1000000.0
half_sentinel = 500000.0
pivot_span = 16.0


def _row_halo(block, dim, width):
    count = lax.axis_size("row")
    forward = [(i, i + 1) for i in range(count - 1)]
    backward = [(target, source) for source, target in forward]
    size = block.shape[dim]
    low = lax.ppermute(lax.slice_in_dim(block, size - width, None, axis=dim), "row", forward)
    high = lax.ppermute(lax.slice_in_dim(block, 0, width, axis=dim), "row", backward)
    return jnp.concatenate([low, block, high], axis=dim)


def _col_halo(block, dim, width):
    count = lax.axis_size("col")
    size = block.shape[dim]
    right_edge = lax.slice_in_dim(block, size - width, None, axis=dim)
    left_edge = lax.slice_in_dim(block, 0, width, axis=dim)
    if count != 2:
        forward = [(i, i + 1) for i in range(count - 1)]
        backward = [(target, source) for source, target in forward]
        low = lax.ppermute(right_edge, "col", forward)
        high = lax.ppermute(left_edge, "col", backward)
        return jnp.concatenate([low, block, high], axis=dim)
    first = lax.axis_index("col") == 0
    outgoing = jnp.moveaxis(jnp.where(first, right_edge, left_edge), dim, 0)
    packed_shape = outgoing.shape
    packed = outgoing.reshape(width, -1)
    arrived = lax.ppermute(packed, "col", [(0, 1), (1, 0)])
    arrived = jnp.moveaxis(arrived.reshape(packed_shape), 0, dim)
    zeros = jnp.zeros_like(arrived)
    low = jnp.where(first, zeros, arrived)
    high = jnp.where(first, arrived, zeros)
    return jnp.concatenate([low, block, high], axis=dim)


def extended(block, row_dim, col_dim, width):
    return _col_halo(_row_halo(block, row_dim, width), col_dim, width)


def lanczos_table():
    fraction = jnp.arange(NFRAC, dtype=jnp.float32) / NFRAC
    offset_grid = jnp.arange(-2, 4, dtype=jnp.float32)
    spread = offset_grid[None, :] - fraction[:, None]
    kernel = jnp.sinc(spread) * jnp.sinc(spread / 3.0)
    return kernel / jnp.sum(kernel, axis=1, keepdims=True)


def blur_table():
    offset_grid = jnp.arange(-PSF_RADIUS, PSF_RADIUS + 1, dtype=jnp.float32)
    widths = 0.7 + 0.2 * jnp.arange(NPSF, dtype=jnp.float32)
    kernel = jnp.exp(-0.5 * (offset_grid[None, :] / widths[:, None]) ** 2)
    return kernel / jnp.sum(kernel, axis=1, keepdims=True)


def lookup(indices, entries, kernel_table):
    chooser = (indices[:, None] == lax.broadcasted_iota(jnp.int32, (1, entries), 1)).astype(
        jnp.float32
    )
    return jnp.dot(chooser, kernel_table, precision=lax.Precision.HIGHEST)


def placed_taps(weights, shifts):
    reach = 2 * HALO + 1
    positions = lax.broadcasted_iota(jnp.int32, (1, 1, reach), 2)
    tap_slot = HALO + shifts[:, None, None] + lax.broadcasted_iota(jnp.int32, (1, 6, 1), 1) - 2
    spread = (tap_slot == positions).astype(jnp.float32)
    return jnp.sum(weights[:, :, None] * spread, axis=1)


def resample_axis(stack, coefficients, out_len, which_axis):
    out_shape = list(stack.shape)
    out_shape[which_axis] = out_len
    total = jnp.zeros(tuple(out_shape), jnp.float32)
    for position in range(2 * HALO + 1):
        window = lax.slice_in_dim(stack, position, position + out_len, 1, which_axis)
        total = total + coefficients[:, position, None, None] * window
    return total


def bisect_lower(valid_count, count_below):

    def one_pass(sweep_no, bounds):
        lower_edge, upper_edge = bounds
        middle = 0.5 * (lower_edge + upper_edge)
        enough = 2.0 * count_below(middle) >= valid_count
        return (jnp.where(enough, lower_edge, middle), jnp.where(enough, middle, upper_edge))

    initial = (
        jnp.full(valid_count.shape, -pivot_span, jnp.float32),
        jnp.full(valid_count.shape, pivot_span, jnp.float32),
    )
    return lax.fori_loop(0, PASSES, one_pass, initial)[0]


def stack_median(pixel_stack):
    valid_count = jnp.sum(pixel_stack < half_sentinel, axis=0, dtype=jnp.float32)

    def count_below(middle):
        return jnp.sum(pixel_stack <= middle[None], axis=0, dtype=jnp.float32)

    lower_edge = bisect_lower(valid_count, count_below)
    return jnp.min(jnp.where(pixel_stack > lower_edge[None], pixel_stack, sentinel), axis=0)


def body(exposures, bad_pixels, offsets, warp_index, blur_index):
    group_size, row_count, col_count = exposures.shape
    kernel_table = lanczos_table()
    coef_down = placed_taps(lookup(warp_index[:, 0], NFRAC, kernel_table), offsets[:, 0])
    coef_across = placed_taps(lookup(warp_index[:, 1], NFRAC, kernel_table), offsets[:, 1])
    padded = extended(exposures, 1, 2, HALO)
    across = resample_axis(padded, coef_down, row_count, 1)
    warped = resample_axis(across, coef_across, col_count, 2)
    flagged = jnp.where(bad_pixels == 1, sentinel, warped)
    band = stack_median(lax.all_to_all(flagged, "exp", split_axis=1, concat_axis=0, tiled=True))
    groups = lax.axis_size("exp")
    median_sky = lax.all_to_all(
        jnp.tile(band, (groups, 1)), "exp", split_axis=0, concat_axis=0, tiled=True
    )
    bordered = extended(median_sky, 0, 1, PSF_RADIUS)
    blur = blur_table()
    taps = 2 * PSF_RADIUS + 1
    blurred_rows = jnp.zeros((NPSF, row_count, col_count + 2 * PSF_RADIUS), jnp.float32)
    for tap_no in range(taps):
        blurred_rows = (
            blurred_rows
            + blur[:, tap_no, None, None] * bordered[None, tap_no : tap_no + row_count, :]
        )
    smoothed = jnp.zeros((NPSF, row_count, col_count), jnp.float32)
    for tap_no in range(taps):
        smoothed = (
            smoothed + blur[:, tap_no, None, None] * blurred_rows[:, :, tap_no : tap_no + col_count]
        )
    chooser = (blur_index[:, None] == lax.broadcasted_iota(jnp.int32, (1, NPSF), 1)).astype(
        jnp.float32
    )
    sky_model = jnp.zeros((group_size, row_count, col_count), jnp.float32)
    for kernel_no in range(NPSF):
        sky_model = sky_model + chooser[:, kernel_no, None, None] * smoothed[kernel_no][None]
    residual = jnp.where(bad_pixels == 1, 0.0, warped - sky_model)
    return (residual, median_sky)


def solution(mesh):
    return jax.shard_map(
        body,
        mesh=mesh,
        in_specs=(
            P("exp", "row", "col"),
            P("exp", "row", "col"),
            P("exp", None),
            P("exp", None),
            P("exp"),
        ),
        out_specs=(P("exp", "row", "col"), P("row", "col")),
        check_vma=False,
    )
```

profile of v0, /device:TPU:0, one launch (start us, length us, event | category | flops | bytes accessed | tf_op | source)
XLA Modules:
  0.0 90.9 jit_solution(72379477720639308)
XLA Ops:
  0.6 1.3 %fusion.134 = (f32[16,11,512]{2,1,0:T(8,128)S(1)}, f32[16,11,512]{2,1,0:T(8,128)S(1)}) fusion(f32[16,32,512]{2,1,0:T(8,128)} %param.8), kind=kLoop, calls=%fused_computation.315 | loop fusion | bytes 1441792 | tf_op jit(solution)/shard_map/slice | solution.py:22
  2.2 3.3 %collective-permute-start = (f32[16,11,512]{2,0,1:T(8,128)S(1)}, f32[16,11,512]{2,0,1:T(8,128)}, u32[]{:S(2)}, u32[]{:S(2)}) collective-permute-start(f32[16,11,512]{2,0,1:T(8,128)S(1)} %copy.47), channel_id=1, source_target_pairs={{0,2},{2,4},{4,6},{1,3},{3,5},{5,7},{8,10},{10,12},{12,14},{9,11},... | collective-permute-start | bytes 1081352 | tf_op jit(solution)/shard_map/ppermute | solution.py:21
  5.7 1.3 %collective-permute-start.1 = (f32[16,11,512]{2,0,1:T(8,128)S(1)}, f32[16,11,512]{2,0,1:T(8,128)S(1)}, u32[]{:S(2)}, u32[]{:S(2)}) collective-permute-start(f32[16,11,512]{2,0,1:T(8,128)S(1)} %copy.48), channel_id=1, source_target_pairs={{2,0},{4,2},{6,4},{3,1},{5,3},{7,5},{10,8},{12,10},{14,12},{11,9},... | collective-permute-start | bytes 1081352 | tf_op jit(solution)/shard_map/ppermute | solution.py:22
  7.7 0.8 slice_reduce_fusion.43
  8.5 1.1 %slice_reduce_fusion.44 = (f32[16]{0:T(128)}, f32[16]{0:T(128)}, f32[16]{0:T(128)}, f32[16]{0:T(128)}, f32[16]{0:T(128)}, /*index=5*/f32[16]{0:T(128)}, f32[16]{...) fusion(f32[16,23]{1,0:T(8,128)S(1)} %select_reduce_fusion), kind=kLoop, calls=%fused_computation.204 | loop fusion | bytes 2432 | tf_op jit(solution)/shard_map/slice | solution.py:89
  9.7 1.1 %slice_reduce_fusion.45 = (f32[16]{0:T(128)S(1)}, f32[16]{0:T(128)S(1)}, f32[16]{0:T(128)}, f32[16]{0:T(128)}, f32[16]{0:T(128)}, /*index=5*/f32[16]{0:T(128)}, ...) fusion(f32[16,23]{1,0:T(8,128)S(1)} %select_reduce_fusion.1), kind=kLoop, calls=%fused_computation.205 | loop fusion | bytes 2432 | tf_op jit(solution)/shard_map/slice | solution.py:89
  10.7 1.0 %constant_dynamic-update-slice_fusion.2 = f32[16,54,512]{2,0,1:T(8,128)S(1)} fusion(f32[16,11,512]{2,0,1:T(8,128)} %collective-permute-done), kind=kLoop, calls=%fused_computation.208 | loop fusion | bytes 720896
  11.8 0.6 constant_dynamic-update-slice_fusion.1
  13.0 2.4 %collective-permute-start.2 = (f32[11,864]{1,0:T(8,128)S(1)}, f32[11,864]{1,0:T(8,128)S(1)}, u32[]{:S(2)}, u32[]{:S(2)}) collective-permute-start(f32[11,864]{1,0:T(8,128)S(1)} %reshape.187), channel_id=1, source_target_pairs={{0,1},{1,0},{2,3},{3,2},{4,5},{5,4},{6,7},{7,6},{8,9},{9,8},{10,11... | collective-permute-start | bytes 114056 | tf_op jit(solution)/shard_map/ppermute | solution.py:41
  15.6 1.9 %collective-permute-done.2 = f32[11,864]{1,0:T(8,128)S(1)} collective-permute-done((f32[11,864]{1,0:T(8,128)S(1)}, f32[11,864]{1,0:T(8,128)S(1)}, u32[]{:S(2)}, u32[]{:S(2)}) %collective-permute-start.2) | collective-permute-done | bytes 38048 | tf_op jit(solution)/shard_map/ppermute | solution.py:41
  17.6 0.3 copy.42
  18.1 0.3 copy.41
  18.6 0.7 pad_maximum_fusion
  19.8 3.9 %fusion = f32[16,32,534]{2,0,1:T(8,128)S(1)} fusion(f32[16,54,534]{2,0,1:T(8,128)S(1)} %pad_maximum_fusion, f32[16]{0:T(128)S(1)} %copy-done.24, f32[16]{0:T(128)S(1)} %copy-done.25, f32[16]{0:T(128)S(1)} %copy-done.26, f32[16]{0:T(128)S(1)} %copy-done.27, f32[16]{0:T(128)S(1)} %copy-done.28, f32[16]{0:T(128)S(1)} %copy-done.29, f32[16]{0:T(128)S(1)} %copy-done.30, ...), kind=kLoop, calls=%fused_computation.8 | loop fusion | flops 12303360 | bytes 26248640 | tf_op jit(solution)/shard_map/add | solution.py:89
  23.8 7.0 %broadcast_select_fusion = (f32[16,32,512]{2,0,1:T(8,128)}, f32[16,32,512]{2,0,1:T(8,128)S(1)}, pred[16,32,512]{2,0,1:T(8,128)(4,1)S(1)}) fusion(f32[16,32,534]{2,0,1:T(8,128)S(1)} %fusion, f32[16]{0:T(128)S(1)} %get-tuple-element.56, f32[16]{0:T(128)S(1)} %copy-done.2, f32[16]{0:T(128)S(1)} %copy-done.3, f32[16]{0:T(128)S(1)} %copy-done.4, ...), kind=kLoop, calls=%fused_computation.119 | loop fusion | flops 12320768 | bytes 27526592 | tf_op jit(solution)/shard_map/jit(_where)/select_n | solution.py:126
  30.8 5.4 %all-to-all-start = ((f32[16,32,512]{2,0,1:T(8,128)}), f32[16,32,512]{2,0,1:T(8,128)S(1)}, u32[]{:S(2)}, u32[]{:S(2)}) async-start(f32[16,32,512]{2,0,1:T(8,128)} %get-tuple-element.113), calls=%async_computation | async-start | bytes 2097152 | tf_op jit(solution)/shard_map/all_to_all | solution.py:127
  36.4 26.2 %all-to-all-done = f32[16,32,512]{2,0,1:T(8,128)S(1)} async-done(((f32[16,32,512]{2,0,1:T(8,128)}), f32[16,32,512]{2,0,1:T(8,128)S(1)}, u32[]{:S(2)}, u32[]{:S(2)}) %all-to-all-start) | async-done | bytes 1048608 | tf_op jit(solution)/shard_map/all_to_all | solution.py:127
  62.6 0.6 copy.43
  63.4 3.6 %while.13 = (s32[]{:T(128)}, f32[8,512]{1,0:T(8,128)S(1)}, f32[8,512]{1,0:T(8,128)S(1)}, f32[64,8,512]{2,1,0:T(8,128)S(1)}, f32[8,512]{1,0:T(8,128)S(1)}, /*index=5*/s32[]{:T(128)}, s32[]{:T(128)}) while((s32[]{:T(128)}, f32[8,512]{1,0:T(8,128)S(1)}, f32[8,512]{1,0:T(8,128)S(1)}, f32[64,8,512]{2,1,0:T(8,128)S(1)}, ...), condition=%wide.region_7.9_spmd.clone, body=%wide.region_5.8_spmd.clone.sunk | while | flops 1110019 | bytes 1302625 | solution.py:105
  67.2 0.6 tile.2
  67.8 3.3 %all-to-all-start.1 = ((f32[4,8,512]{2,1,0:T(8,128)}), f32[4,8,512]{2,1,0:T(8,128)S(1)}, u32[]{:S(2)}, u32[]{:S(2)}) async-start(f32[4,8,512]{2,1,0:T(8,128)} %tile.2), calls=%async_computation.1 | async-start | bytes 131072 | tf_op jit(solution)/shard_map/all_to_all | solution.py:129
  71.1 5.8 %all-to-all-done.1 = f32[4,8,512]{2,1,0:T(8,128)S(1)} async-done(((f32[4,8,512]{2,1,0:T(8,128)}), f32[4,8,512]{2,1,0:T(8,128)S(1)}, u32[]{:S(2)}, u32[]{:S(2)}) %all-to-all-start.1) | async-done | bytes 65568 | tf_op jit(solution)/shard_map/all_to_all | solution.py:129
  76.9 1.3 %collective-permute-start.4 = (f32[4,512]{1,0:T(4,128)S(1)}, f32[4,512]{1,0:T(4,128)S(1)}, u32[]{:S(2)}, u32[]{:S(2)}) collective-permute-start(f32[4,512]{1,0:T(4,128)S(1)} %get-tuple-element.136), channel_id=1, source_target_pairs={{2,0},{4,2},{6,4},{3,1},{5,3},{7,5},{10,8},{12,10},{14,12},{11,9},... | collective-permute-start | bytes 24584 | tf_op jit(solution)/shard_map/ppermute | solution.py:22
  78.2 3.2 %collective-permute-start.3 = (f32[4,512]{1,0:T(4,128)S(1)}, f32[4,512]{1,0:T(4,128)S(1)}, u32[]{:S(2)}, u32[]{:S(2)}) collective-permute-start(f32[4,512]{1,0:T(4,128)S(1)} %get-tuple-element.135), channel_id=1, source_target_pairs={{0,2},{2,4},{4,6},{1,3},{3,5},{5,7},{8,10},{10,12},{12,14},{9,11},... | collective-permute-start | bytes 24584 | tf_op jit(solution)/shard_map/ppermute | solution.py:21
  81.5 0.6 collective-permute-done.3
  82.1 1.5 %collective-permute-start.5 = (f32[4,40]{0,1:T(8,128)S(1)}, f32[4,40]{0,1:T(8,128)S(1)}, u32[]{:S(2)}, u32[]{:S(2)}) collective-permute-start(f32[4,40]{0,1:T(8,128)S(1)} %fusion.55), channel_id=1, source_target_pairs={{0,1},{1,0},{2,3},{3,2},{4,5},{5,4},{6,7},{7,6},{8,9},{9,8},{10,11... | collective-permute-start | bytes 1928 | tf_op jit(solution)/shard_map/ppermute | solution.py:41
  83.7 2.3 %collective-permute-done.5 = f32[4,40]{0,1:T(8,128)S(1)} collective-permute-done((f32[4,40]{0,1:T(8,128)S(1)}, f32[4,40]{0,1:T(8,128)S(1)}, u32[]{:S(2)}, u32[]{:S(2)}) %collective-permute-start.5) | collective-permute-done | bytes 672 | tf_op jit(solution)/shard_map/ppermute | solution.py:41
  86.1 0.6 multiply_add_fusion
  86.7 1.3 %fusion.45 = f32[8,32,512]{2,1,0:T(8,128)S(1)} fusion(f32[8,32,520]{2,1,0:T(8,128)S(1)} %multiply_add_fusion, f32[8]{0:T(128)S(1)} %get-tuple-element.142, f32[8]{0:T(128)S(1)} %get-tuple-element.143, f32[8]{0:T(128)S(1)} %get-tuple-element.144, f32[8]{0:T(128)S(1)} %get-tuple-element.145, f32[8]{0:T(128)S(1)} %get-tuple-element.146, ...), kind=kLoop, calls=%fused_computation.103 | loop fusion | flops 2228224 | bytes 5243168 | tf_op jit(solution)/shard_map/add | solution.py:144
  88.0 0.7 subtract_select_fusion
  88.7 1.6 %copy.44 = f32[16,32,512]{2,1,0:T(8,128)} copy(f32[16,32,512]{2,0,1:T(8,128)S(1)} %subtract_select_fusion) | data formatting | bytes 2097152
  90.3 0.6 copy.62
  (208 shorter events, 6.1 us)
Async XLA Ops:
  2.0 5.1 %copy-start.41 = (s32[16,2]{0,1:T(2,128)S(1)}, s32[16,2]{0,1:T(2,128)}, u32[]{:S(2)}) copy-start(s32[16,2]{0,1:T(2,128)} %param.11) | copy-start | bytes 388
  2.0 5.1 %copy-start.42 = (s32[16,2]{0,1:T(2,128)S(1)}, s32[16,2]{0,1:T(2,128)}, u32[]{:S(2)}) copy-start(s32[16,2]{0,1:T(2,128)} %param.10) | copy-start | bytes 388
  2.2 9.6 %copy-start = (f32[16,32,512]{2,1,0:T(8,128)S(1)}, f32[16,32,512]{2,1,0:T(8,128)}, u32[]{:S(2)}) copy-start(f32[16,32,512]{2,1,0:T(8,128)} %param.8) | copy-start | bytes 3145732
  2.2 8.5 %collective-permute-start = (f32[16,11,512]{2,0,1:T(8,128)S(1)}, f32[16,11,512]{2,0,1:T(8,128)}, u32[]{:S(2)}, u32[]{:S(2)}) collective-permute-start(f32[16,11,512]{2,0,1:T(8,128)S(1)} %copy.47), channel_id=1, source_target_pairs={{0,2},{2,4},{4,6},{1,3},{3,5},{5,7},{8,10},{10,12},{12,14},{9,11},... | collective-permute-start | bytes 1081352 | tf_op jit(solution)/shard_map/ppermute | solution.py:21
  5.7 6.7 %collective-permute-start.1 = (f32[16,11,512]{2,0,1:T(8,128)S(1)}, f32[16,11,512]{2,0,1:T(8,128)S(1)}, u32[]{:S(2)}, u32[]{:S(2)}) collective-permute-start(f32[16,11,512]{2,0,1:T(8,128)S(1)} %copy.48), channel_id=1, source_target_pairs={{2,0},{4,2},{6,4},{3,1},{5,3},{7,5},{10,8},{12,10},{14,12},{11,9},... | collective-permute-start | bytes 1081352 | tf_op jit(solution)/shard_map/ppermute | solution.py:22
  13.0 4.5 %collective-permute-start.2 = (f32[11,864]{1,0:T(8,128)S(1)}, f32[11,864]{1,0:T(8,128)S(1)}, u32[]{:S(2)}, u32[]{:S(2)}) collective-permute-start(f32[11,864]{1,0:T(8,128)S(1)} %reshape.187), channel_id=1, source_target_pairs={{0,1},{1,0},{2,3},{3,2},{4,5},{5,4},{6,7},{7,6},{8,9},{9,8},{10,11... | collective-permute-start | bytes 114056 | tf_op jit(solution)/shard_map/ppermute | solution.py:41
  18.4 1.0 %copy-start.19 = (f32[16]{0:T(128)S(1)}, f32[16]{0:T(128)}, u32[]{:S(2)}) copy-start(f32[16]{0:T(128)} %get-tuple-element.97) | copy-start | bytes 196
  18.4 1.0 %copy-start.20 = (f32[16]{0:T(128)S(1)}, f32[16]{0:T(128)}, u32[]{:S(2)}) copy-start(f32[16]{0:T(128)} %get-tuple-element.98) | copy-start | bytes 196
  19.6 4.0 %copy-start.1 = (s32[16,32,512]{2,1,0:T(8,128)S(1)}, s32[16,32,512]{2,1,0:T(8,128)}, u32[]{:S(2)}) copy-start(s32[16,32,512]{2,1,0:T(8,128)} %param.9) | copy-start | bytes 3145732
  19.6 4.0 %copy-start.2 = (f32[16]{0:T(128)S(1)}, f32[16]{0:T(128)}, u32[]{:S(2)}) copy-start(f32[16]{0:T(128)} %get-tuple-element.57) | copy-start | bytes 196
  19.6 4.0 %copy-start.3 = (f32[16]{0:T(128)S(1)}, f32[16]{0:T(128)}, u32[]{:S(2)}) copy-start(f32[16]{0:T(128)} %get-tuple-element.58) | copy-start | bytes 196
  19.6 4.0 %copy-start.4 = (f32[16]{0:T(128)S(1)}, f32[16]{0:T(128)}, u32[]{:S(2)}) copy-start(f32[16]{0:T(128)} %get-tuple-element.59) | copy-start | bytes 196
  19.6 4.0 %copy-start.5 = (f32[16]{0:T(128)S(1)}, f32[16]{0:T(128)}, u32[]{:S(2)}) copy-start(f32[16]{0:T(128)} %get-tuple-element.60) | copy-start | bytes 196
  19.6 4.0 %copy-start.6 = (f32[16]{0:T(128)S(1)}, f32[16]{0:T(128)}, u32[]{:S(2)}) copy-start(f32[16]{0:T(128)} %get-tuple-element.61) | copy-start | bytes 196
  19.6 4.0 %copy-start.7 = (f32[16]{0:T(128)S(1)}, f32[16]{0:T(128)}, u32[]{:S(2)}) copy-start(f32[16]{0:T(128)} %get-tuple-element.62) | copy-start | bytes 196
  19.7 4.0 %copy-start.8 = (f32[16]{0:T(128)S(1)}, f32[16]{0:T(128)}, u32[]{:S(2)}) copy-start(f32[16]{0:T(128)} %get-tuple-element.63) | copy-start | bytes 196
  19.7 4.0 %copy-start.9 = (f32[16]{0:T(128)S(1)}, f32[16]{0:T(128)}, u32[]{:S(2)}) copy-start(f32[16]{0:T(128)} %get-tuple-element.64) | copy-start | bytes 196
  19.7 4.0 %copy-start.10 = (f32[16]{0:T(128)S(1)}, f32[16]{0:T(128)}, u32[]{:S(2)}) copy-start(f32[16]{0:T(128)} %get-tuple-element.65) | copy-start | bytes 196
  19.7 4.0 %copy-start.11 = (f32[16]{0:T(128)S(1)}, f32[16]{0:T(128)}, u32[]{:S(2)}) copy-start(f32[16]{0:T(128)} %get-tuple-element.66) | copy-start | bytes 196
  19.7 4.0 %copy-start.12 = (f32[16]{0:T(128)S(1)}, f32[16]{0:T(128)}, u32[]{:S(2)}) copy-start(f32[16]{0:T(128)} %get-tuple-element.67) | copy-start | bytes 196
  19.7 4.0 %copy-start.13 = (f32[16]{0:T(128)S(1)}, f32[16]{0:T(128)}, u32[]{:S(2)}) copy-start(f32[16]{0:T(128)} %get-tuple-element.68) | copy-start | bytes 196
  19.7 4.0 %copy-start.14 = (f32[16]{0:T(128)S(1)}, f32[16]{0:T(128)}, u32[]{:S(2)}) copy-start(f32[16]{0:T(128)} %get-tuple-element.69) | copy-start | bytes 196
  19.7 4.0 %copy-start.15 = (f32[16]{0:T(128)S(1)}, f32[16]{0:T(128)}, u32[]{:S(2)}) copy-start(f32[16]{0:T(128)} %get-tuple-element.70) | copy-start | bytes 196
  19.7 4.0 %copy-start.16 = (f32[16]{0:T(128)S(1)}, f32[16]{0:T(128)}, u32[]{:S(2)}) copy-start(f32[16]{0:T(128)} %get-tuple-element.71) | copy-start | bytes 196
  19.7 4.0 %copy-start.17 = (f32[16]{0:T(128)S(1)}, f32[16]{0:T(128)}, u32[]{:S(2)}) copy-start(f32[16]{0:T(128)} %get-tuple-element.72) | copy-start | bytes 196
  19.8 4.0 %copy-start.18 = (f32[16]{0:T(128)S(1)}, f32[16]{0:T(128)}, u32[]{:S(2)}) copy-start(f32[16]{0:T(128)} %get-tuple-element.73) | copy-start | bytes 196
  30.8 31.8 %all-to-all-start = ((f32[16,32,512]{2,0,1:T(8,128)}), f32[16,32,512]{2,0,1:T(8,128)S(1)}, u32[]{:S(2)}, u32[]{:S(2)}) async-start(f32[16,32,512]{2,0,1:T(8,128)} %get-tuple-element.113), calls=%async_computation | async-start | bytes 2097152 | tf_op jit(solution)/shard_map/all_to_all | solution.py:127
  67.0 14.4 %copy-start.43 = (s32[16]{0:T(128)S(1)}, s32[16]{0:T(128)}, u32[]{:S(2)}) copy-start(s32[16]{0:T(128)} %param.12) | copy-start | bytes 196
  67.8 9.1 %all-to-all-start.1 = ((f32[4,8,512]{2,1,0:T(8,128)}), f32[4,8,512]{2,1,0:T(8,128)S(1)}, u32[]{:S(2)}, u32[]{:S(2)}) async-start(f32[4,8,512]{2,1,0:T(8,128)} %tile.2), calls=%async_computation.1 | async-start | bytes 131072 | tf_op jit(solution)/shard_map/all_to_all | solution.py:129
  76.9 4.5 %collective-permute-start.4 = (f32[4,512]{1,0:T(4,128)S(1)}, f32[4,512]{1,0:T(4,128)S(1)}, u32[]{:S(2)}, u32[]{:S(2)}) collective-permute-start(f32[4,512]{1,0:T(4,128)S(1)} %get-tuple-element.136), channel_id=1, source_target_pairs={{2,0},{4,2},{6,4},{3,1},{5,3},{7,5},{10,8},{12,10},{14,12},{11,9},... | collective-permute-start | bytes 24584 | tf_op jit(solution)/shard_map/ppermute | solution.py:22
  78.2 3.8 %collective-permute-start.3 = (f32[4,512]{1,0:T(4,128)S(1)}, f32[4,512]{1,0:T(4,128)S(1)}, u32[]{:S(2)}, u32[]{:S(2)}) collective-permute-start(f32[4,512]{1,0:T(4,128)S(1)} %get-tuple-element.135), channel_id=1, source_target_pairs={{0,2},{2,4},{4,6},{1,3},{3,5},{5,7},{8,10},{10,12},{12,14},{9,11},... | collective-permute-start | bytes 24584 | tf_op jit(solution)/shard_map/ppermute | solution.py:21
  82.1 3.8 %collective-permute-start.5 = (f32[4,40]{0,1:T(8,128)S(1)}, f32[4,40]{0,1:T(8,128)S(1)}, u32[]{:S(2)}, u32[]{:S(2)}) collective-permute-start(f32[4,40]{0,1:T(8,128)S(1)} %fusion.55), channel_id=1, source_target_pairs={{0,1},{1,0},{2,3},{3,2},{4,5},{5,4},{6,7},{7,6},{8,9},{9,8},{10,11... | collective-permute-start | bytes 1928 | tf_op jit(solution)/shard_map/ppermute | solution.py:41
  (20 other events, 19.5 us)
where the time goes:
time: 91.4 us; the launch traced here: 90.9 us
  waiting for transfers between devices  36.9 us (40%)
  starting transfers between devices  21.6 us (24%)
  other arithmetic  18.2 us (20%)
  local copies, waits for them, and re-layouts  11.5 us (13%)
  between operations  1.6 us (2%)
    all_to_all x1, waiting for transfers between devices, body(): lax.all_to_all(flagged, 'exp', split_axis=1, concat_axis=0, tiled=True)  26.2 us
    select_n x1, other arithmetic, body(): flagged = jnp.where(bad_pixels == 1, sentinel, warped)  6.99 us
    ppermute x2, starting transfers between devices, _row_halo(): lax.ppermute(lax.slice_in_dim(block, size - width, None, axis=dim), 'row'...  6.48 us
    all_to_all x1, waiting for transfers between devices, body(): lax.all_to_all(jnp.tile(band, (groups, 1)), 'exp', split_axis=0, concat_a...  5.8 us
    all_to_all x1, starting transfers between devices, body(): lax.all_to_all(flagged, 'exp', split_axis=1, concat_axis=0, tiled=True)  5.4 us
    unnamed x94, local copies, waits for them, and re-layouts  4.46 us
    ppermute x2, waiting for transfers between devices, _col_halo(): arrived = lax.ppermute(packed, 'col', [(0, 1), (1, 0)])  4.23 us
    ppermute x2, starting transfers between devices, _col_halo(): arrived = lax.ppermute(packed, 'col', [(0, 1), (1, 0)])  3.87 us
  transfers between devices with their start and end apart: 8, of which 5 were waited for; matrix products, arithmetic and copies ran while one was open for 7% of the time, Pallas kernels for 0%

commit v1 on v0

--- a/solution.py
+++ b/solution.py
@@ -124,7 +124,14 @@
     across = resample_axis(padded, coef_down, row_count, 1)
     warped = resample_axis(across, coef_across, col_count, 2)
     flagged = jnp.where(bad_pixels == 1, sentinel, warped)
-    band = stack_median(lax.all_to_all(flagged, "exp", split_axis=1, concat_axis=0, tiled=True))
+    band = stack_median(
+        jnp.concatenate(
+            lax.all_to_all(
+                jnp.stack(jnp.split(flagged, lax.axis_size("exp"), axis=1)), "exp", 0, 0
+            ),
+            axis=0,
+        )
+    )
     groups = lax.axis_size("exp")
     median_sky = lax.all_to_all(
         jnp.tile(band, (groups, 1)), "exp", split_axis=0, concat_axis=0, tiled=True

time: 91.4 us -> 88.3 us (0.966)
  local copies, waits for them, and re-layouts: 11.5 us -> 5.44 us
  other arithmetic: 18.2 us -> 21.5 us
    unnamed x94 -> x11, local copies, waits for them, and re-layouts: 4.46 us -> 0.65 us
    slice x4, local copies, waits for them, and re-layouts: 3.13 us -> 1.41 us  [resample_axis(): total = total + coefficients[:, position, None, None] * window]
    slice x1 -> x2, local copies, waits for them, and re-layouts: 0.01 us -> 1.4 us  [_row_halo(): lax.slice_in_dim(block, size - width, None, axis=dim)]
    slice x1 -> x0, local copies, waits for them, and re-layouts: 1.32 us -> none  [_row_halo(): lax.slice_in_dim(block, 0, width, axis=dim)]
    select_n x1, other arithmetic: 0.72 us -> 1.77 us  [body(): residual = jnp.where(bad_pixels == 1, 0.0, warped - sky_model)]
    another operation x0 -> x1, other arithmetic: none -> 1.04 us  [body(): jnp.stack(jnp.split(flagged, lax.axis_size('exp'), axis=1))]
  transfers between devices with their start and end apart: 8 -> 8, of which waited for: 5 -> 5; matrix products, arithmetic and copies ran while one was open for 7% -> 3% of each run, Pallas kernels for 0% -> 0%
where the time goes in v1:
time: 88.3 us; the launch traced here: 87.9 us
  waiting for transfers between devices  36.8 us (42%)
  starting transfers between devices  22.1 us (25%)
  other arithmetic  21.5 us (24%)
  local copies, waits for them, and re-layouts  5.44 us (6%)
  between operations  0.97 us (1%)
    all_to_all x1, waiting for transfers between devices, body(): lax.all_to_all(jnp.stack(jnp.split(flagged, lax.axis_size('exp'), axis=1)...  25.9 us
    select_n x1, other arithmetic, body(): flagged = jnp.where(bad_pixels == 1, sentinel, warped)  7.57 us
    ppermute x2, starting transfers between devices, _row_halo(): lax.ppermute(lax.slice_in_dim(block, size - width, None, axis=dim), 'row'...  6.27 us
    all_to_all x1, waiting for transfers between devices, body(): lax.all_to_all(jnp.tile(band, (groups, 1)), 'exp', split_axis=0, concat_a...  5.87 us
    all_to_all x1, starting transfers between devices, body(): lax.all_to_all(jnp.stack(jnp.split(flagged, lax.axis_size('exp'), axis=1)...  5.4 us
    ppermute x2, starting transfers between devices, _col_halo(): arrived = lax.ppermute(packed, 'col', [(0, 1), (1, 0)])  4.53 us
    ppermute x2, waiting for transfers between devices, _col_halo(): arrived = lax.ppermute(packed, 'col', [(0, 1), (1, 0)])  4.4 us
    add x1, other arithmetic, resample_axis(): total = total + coefficients[:, position, None, None] * window  4.15 us
  transfers between devices with their start and end apart: 8, of which 5 were waited for; matrix products, arithmetic and copies ran while one was open for 3% of the time, Pallas kernels for 0%

profile of v1, /device:TPU:0, one launch (start us, length us, event | category | flops | bytes accessed | tf_op | source)
XLA Modules:
  0.0 87.9 jit_solution(4788347216591767285)
XLA Ops:
  0.7 1.4 %fusion.135 = (f32[16,11,512]{2,1,0:T(8,128)S(1)}, f32[16,11,512]{2,1,0:T(8,128)S(1)}) fusion(f32[16,32,512]{2,1,0:T(8,128)} %param.8), kind=kLoop, calls=%fused_computation.319 | loop fusion | bytes 1441792 | tf_op jit(solution)/shard_map/slice | solution.py:21
  2.1 1.3 %collective-permute-start.1 = (f32[16,11,512]{2,1,0:T(8,128)S(1)}, f32[16,11,512]{2,1,0:T(8,128)S(1)}, u32[]{:S(2)}, u32[]{:S(2)}) collective-permute-start(f32[16,11,512]{2,1,0:T(8,128)S(1)} %get-tuple-element.115), channel_id=1, source_target_pairs={{2,0},{4,2},{6,4},{3,1},{5,3},{7,5},{10,8},{12,10},{14,12},{11,9},... | collective-permute-start | bytes 1081352 | tf_op jit(solution)/shard_map/ppermute | solution.py:22
  3.4 3.1 %collective-permute-start = (f32[16,11,512]{2,1,0:T(8,128)S(1)}, f32[16,11,512]{2,1,0:T(8,128)S(1)}, u32[]{:S(2)}, u32[]{:S(2)}) collective-permute-start(f32[16,11,512]{2,1,0:T(8,128)S(1)} %get-tuple-element.114), channel_id=1, source_target_pairs={{0,2},{2,4},{4,6},{1,3},{3,5},{5,7},{8,10},{10,12},{12,14},{9,11},... | collective-permute-start | bytes 1081352 | tf_op jit(solution)/shard_map/ppermute | solution.py:21
  6.8 0.2 fusion.67
  7.2 0.2 slice_reduce_fusion.43
  7.4 0.5 slice_reduce_fusion.44
  8.0 0.5 slice_reduce_fusion.45
  8.5 0.2 fusion.54
  8.7 0.2 copy.17
  9.1 3.0 %collective-permute-start.2 = (f32[11,864]{1,0:T(8,128)S(1)}, f32[11,864]{1,0:T(8,128)S(1)}, u32[]{:S(2)}, u32[]{:S(2)}) collective-permute-start(f32[11,864]{1,0:T(8,128)S(1)} %reshape.190), channel_id=1, source_target_pairs={{0,1},{1,0},{2,3},{3,2},{4,5},{5,4},{6,7},{7,6},{8,9},{9,8},{10,11... | collective-permute-start | bytes 114056 | tf_op jit(solution)/shard_map/ppermute | solution.py:41
  12.3 1.9 %collective-permute-done.2 = f32[11,864]{1,0:T(8,128)S(1)} collective-permute-done((f32[11,864]{1,0:T(8,128)S(1)}, f32[11,864]{1,0:T(8,128)S(1)}, u32[]{:S(2)}, u32[]{:S(2)}) %collective-permute-start.2) | collective-permute-done | bytes 38048 | tf_op jit(solution)/shard_map/ppermute | solution.py:41
  14.4 0.3 copy.19
  14.8 0.3 copy.18
  15.0 1.0 %pad_maximum_fusion = f32[16,54,534]{2,1,0:T(8,128)S(1)} fusion(f32[16,54,11]{2,1,0:T(8,128)S(1)} %copy.19, f32[16,11,512]{2,1,0:T(8,128)S(1)} %collective-permute-done.1, f32[16,32,512]{2,1,0:T(8,128)S(1)} %copy-done, f32[16,11,512]{2,1,0:T(8,128)S(1)} %collective-permute-done, f32[16,54,11]{2,1,0:T(8,128)S(1)} %copy.18), kind=kLoop, calls=%fused_computation.6 | loop fusion | flops 1845504 | bytes 3691008 | tf_op jit(solution)/shard_map/concatenate | solution.py:46
  16.1 4.1 %fusion = f32[16,32,534]{2,1,0:T(8,128)S(1)} fusion(f32[16,54,534]{2,1,0:T(8,128)S(1)} %pad_maximum_fusion, f32[16]{0:T(128)S(1)} %get-tuple-element.73, f32[16]{0:T(128)S(1)} %get-tuple-element.74, f32[16]{0:T(128)S(1)} %get-tuple-element.75, f32[16]{0:T(128)S(1)} %get-tuple-element.76, f32[16]{0:T(128)S(1)} %get-tuple-element.77, ...), kind=kLoop, calls=%fused_computation.8 | loop fusion | flops 12303360 | bytes 26248640 | tf_op jit(solution)/shard_map/add | solution.py:89
  20.3 7.6 %broadcast_select_fusion = (f32[16,32,512]{2,1,0:T(8,128)S(1)}, f32[16,32,512]{2,1,0:T(8,128)S(1)}, pred[16,32,512]{2,1,0:T(8,128)(4,1)S(1)}) fusion(f32[16,32,534]{2,1,0:T(8,128)S(1)} %fusion, f32[16]{0:T(128)S(1)} %get-tuple-element.50, f32[16]{0:T(128)S(1)} %get-tuple-element.51, f32[16]{0:T(128)S(1)} %get-tuple-element.52, f32[16]{0:T(128)S(1)} %get-tuple-element.53, ...), kind=kLoop, calls=%fused_computation.119 | loop fusion | flops 12320768 | bytes 27526592 | tf_op jit(solution)/shard_map/jit(_where)/select_n | solution.py:126
  27.9 1.0 %pad_maximum_fusion.1 = f32[4,16,8,512]{3,2,1,0:T(8,128)} fusion(f32[1,16,8,512]{3,2,1,0:T(8,128)S(1)} %get-tuple-element.111, f32[1,16,8,512]{3,2,1,0:T(8,128)S(1)} %get-tuple-element.112, f32[1,16,8,512]{3,2,1,0:T(8,128)S(1)} %get-tuple-element.113, f32[1,16,8,512]{3,2,1,0:T(8,128)S(1)} %get-tuple-element.110), kind=kLoop, calls=%fused_computation.98 | loop fusion | flops 786432 | bytes 2097152 | tf_op jit(solution)/shard_map/stack | solution.py:130
  29.0 5.4 %all-to-all-start = ((f32[4,16,8,512]{3,2,1,0:T(8,128)}), f32[4,16,8,512]{3,2,1,0:T(8,128)S(1)}, u32[]{:S(2)}, u32[]{:S(2)}) async-start(f32[4,16,8,512]{3,2,1,0:T(8,128)} %pad_maximum_fusion.1), calls=%async_computation | async-start | bytes 2097152 | tf_op jit(solution)/shard_map/all_to_all | solution.py:129
  34.6 25.9 %all-to-all-done = f32[4,16,8,512]{3,2,1,0:T(8,128)S(1)} async-done(((f32[4,16,8,512]{3,2,1,0:T(8,128)}), f32[4,16,8,512]{3,2,1,0:T(8,128)S(1)}, u32[]{:S(2)}, u32[]{:S(2)}) %all-to-all-start) | async-done | bytes 1048608 | tf_op jit(solution)/shard_map/all_to_all | solution.py:129
  60.7 3.6 %while.13 = (s32[]{:T(128)}, f32[8,512]{1,0:T(8,128)S(1)}, f32[8,512]{1,0:T(8,128)S(1)}, f32[64,8,512]{2,1,0:T(8,128)S(1)}, f32[8,512]{1,0:T(8,128)S(1)}, /*index=5*/s32[]{:T(128)}, s32[]{:T(128)}) while((s32[]{:T(128)}, f32[8,512]{1,0:T(8,128)S(1)}, f32[8,512]{1,0:T(8,128)S(1)}, f32[64,8,512]{2,1,0:T(8,128)S(1)}, ...), condition=%wide.region_7.9_spmd.clone, body=%wide.region_5.8_spmd.clone.sunk | while | flops 1110019 | bytes 1302625 | solution.py:105
  64.5 0.6 tile.2
  65.1 3.3 %all-to-all-start.1 = ((f32[4,8,512]{2,1,0:T(8,128)}), f32[4,8,512]{2,1,0:T(8,128)S(1)}, u32[]{:S(2)}, u32[]{:S(2)}) async-start(f32[4,8,512]{2,1,0:T(8,128)} %tile.2), calls=%async_computation.1 | async-start | bytes 131072 | tf_op jit(solution)/shard_map/all_to_all | solution.py:136
  68.4 5.9 %all-to-all-done.1 = f32[4,8,512]{2,1,0:T(8,128)S(1)} async-done(((f32[4,8,512]{2,1,0:T(8,128)}), f32[4,8,512]{2,1,0:T(8,128)S(1)}, u32[]{:S(2)}, u32[]{:S(2)}) %all-to-all-start.1) | async-done | bytes 65568 | tf_op jit(solution)/shard_map/all_to_all | solution.py:136
  74.3 1.3 %collective-permute-start.4 = (f32[4,512]{1,0:T(4,128)S(1)}, f32[4,512]{1,0:T(4,128)S(1)}, u32[]{:S(2)}, u32[]{:S(2)}) collective-permute-start(f32[4,512]{1,0:T(4,128)S(1)} %get-tuple-element.134), channel_id=1, source_target_pairs={{2,0},{4,2},{6,4},{3,1},{5,3},{7,5},{10,8},{12,10},{14,12},{11,9},... | collective-permute-start | bytes 24584 | tf_op jit(solution)/shard_map/ppermute | solution.py:22
  75.6 3.2 %collective-permute-start.3 = (f32[4,512]{1,0:T(4,128)S(1)}, f32[4,512]{1,0:T(4,128)S(1)}, u32[]{:S(2)}, u32[]{:S(2)}) collective-permute-start(f32[4,512]{1,0:T(4,128)S(1)} %get-tuple-element.133), channel_id=1, source_target_pairs={{0,2},{2,4},{4,6},{1,3},{3,5},{5,7},{8,10},{10,12},{12,14},{9,11},... | collective-permute-start | bytes 24584 | tf_op jit(solution)/shard_map/ppermute | solution.py:21
  78.8 0.6 collective-permute-done.3
  79.5 1.5 %collective-permute-start.5 = (f32[4,40]{0,1:T(8,128)S(1)}, f32[4,40]{0,1:T(8,128)S(1)}, u32[]{:S(2)}, u32[]{:S(2)}) collective-permute-start(f32[4,40]{0,1:T(8,128)S(1)} %fusion.56), channel_id=1, source_target_pairs={{0,1},{1,0},{2,3},{3,2},{4,5},{5,4},{6,7},{7,6},{8,9},{9,8},{10,11... | collective-permute-start | bytes 1928 | tf_op jit(solution)/shard_map/ppermute | solution.py:41
  81.0 2.5 %collective-permute-done.5 = f32[4,40]{0,1:T(8,128)S(1)} collective-permute-done((f32[4,40]{0,1:T(8,128)S(1)}, f32[4,40]{0,1:T(8,128)S(1)}, u32[]{:S(2)}, u32[]{:S(2)}) %collective-permute-start.5) | collective-permute-done | bytes 672 | tf_op jit(solution)/shard_map/ppermute | solution.py:41
  83.6 0.6 multiply_add_fusion
  84.2 1.3 %fusion.45 = f32[8,32,512]{2,1,0:T(8,128)S(1)} fusion(f32[8,32,520]{2,1,0:T(8,128)S(1)} %multiply_add_fusion, f32[8]{0:T(128)S(1)} %get-tuple-element.140, f32[8]{0:T(128)S(1)} %get-tuple-element.141, f32[8]{0:T(128)S(1)} %get-tuple-element.142, f32[8]{0:T(128)S(1)} %get-tuple-element.143, f32[8]{0:T(128)S(1)} %get-tuple-element.144, ...), kind=kLoop, calls=%fused_computation.103 | loop fusion | flops 2228224 | bytes 5243168 | tf_op jit(solution)/shard_map/add | solution.py:151
  85.5 1.8 %subtract_select_fusion = f32[16,32,512]{2,1,0:T(8,128)} fusion(pred[16,32,512]{2,1,0:T(8,128)(4,1)S(1)} %get-tuple-element.109, f32[16,32,512]{2,1,0:T(8,128)S(1)} %get-tuple-element.108, f32[32,512]{1,0:T(8,128)S(1)} %get-tuple-element.117, f32[16]{0:T(128)S(1)} %get-tuple-element.149, f32[32,512]{1,0:T(8,128)S(1)} %get-tuple-element.118, ...), kind=kLoop, calls=%fused_computation.99 | loop fusion | flops 4456448 | bytes 2884096 | tf_op jit(solution)/shard_map/jit(_where)/select_n | solution.py:159
  87.3 0.6 copy.30
  (125 shorter events, 4.9 us)
Async XLA Ops:
  0.6 7.9 %copy-start = (f32[16,32,512]{2,1,0:T(8,128)S(1)}, f32[16,32,512]{2,1,0:T(8,128)}, u32[]{:S(2)}) copy-start(f32[16,32,512]{2,1,0:T(8,128)} %param.8) | copy-start | bytes 3145732
  0.6 5.8 %copy-start.2 = (s32[16,2]{0,1:T(2,128)S(1)}, s32[16,2]{0,1:T(2,128)}, u32[]{:S(2)}) copy-start(s32[16,2]{0,1:T(2,128)} %param.11) | copy-start | bytes 388
  0.6 5.8 %copy-start.3 = (s32[16,2]{0,1:T(2,128)S(1)}, s32[16,2]{0,1:T(2,128)}, u32[]{:S(2)}) copy-start(s32[16,2]{0,1:T(2,128)} %param.10) | copy-start | bytes 388
  2.1 6.4 %collective-permute-start.1 = (f32[16,11,512]{2,1,0:T(8,128)S(1)}, f32[16,11,512]{2,1,0:T(8,128)S(1)}, u32[]{:S(2)}, u32[]{:S(2)}) collective-permute-start(f32[16,11,512]{2,1,0:T(8,128)S(1)} %get-tuple-element.115), channel_id=1, source_target_pairs={{2,0},{4,2},{6,4},{3,1},{5,3},{7,5},{10,8},{12,10},{14,12},{11,9},... | collective-permute-start | bytes 1081352 | tf_op jit(solution)/shard_map/ppermute | solution.py:22
  3.4 5.1 %collective-permute-start = (f32[16,11,512]{2,1,0:T(8,128)S(1)}, f32[16,11,512]{2,1,0:T(8,128)S(1)}, u32[]{:S(2)}, u32[]{:S(2)}) collective-permute-start(f32[16,11,512]{2,1,0:T(8,128)S(1)} %get-tuple-element.114), channel_id=1, source_target_pairs={{0,2},{2,4},{4,6},{1,3},{3,5},{5,7},{8,10},{10,12},{12,14},{9,11},... | collective-permute-start | bytes 1081352 | tf_op jit(solution)/shard_map/ppermute | solution.py:21
  9.1 5.2 %collective-permute-start.2 = (f32[11,864]{1,0:T(8,128)S(1)}, f32[11,864]{1,0:T(8,128)S(1)}, u32[]{:S(2)}, u32[]{:S(2)}) collective-permute-start(f32[11,864]{1,0:T(8,128)S(1)} %reshape.190), channel_id=1, source_target_pairs={{0,1},{1,0},{2,3},{3,2},{4,5},{5,4},{6,7},{7,6},{8,9},{9,8},{10,11... | collective-permute-start | bytes 114056 | tf_op jit(solution)/shard_map/ppermute | solution.py:41
  16.1 4.2 %copy-start.1 = (s32[16,32,512]{2,1,0:T(8,128)S(1)}, s32[16,32,512]{2,1,0:T(8,128)}, u32[]{:S(2)}) copy-start(s32[16,32,512]{2,1,0:T(8,128)} %param.9) | copy-start | bytes 3145732
  29.0 31.5 %all-to-all-start = ((f32[4,16,8,512]{3,2,1,0:T(8,128)}), f32[4,16,8,512]{3,2,1,0:T(8,128)S(1)}, u32[]{:S(2)}, u32[]{:S(2)}) async-start(f32[4,16,8,512]{3,2,1,0:T(8,128)} %pad_maximum_fusion.1), calls=%async_computation | async-start | bytes 2097152 | tf_op jit(solution)/shard_map/all_to_all | solution.py:129
  64.3 14.5 %copy-start.4 = (s32[16]{0:T(128)S(1)}, s32[16]{0:T(128)}, u32[]{:S(2)}) copy-start(s32[16]{0:T(128)} %param.12) | copy-start | bytes 196
  65.1 9.2 %all-to-all-start.1 = ((f32[4,8,512]{2,1,0:T(8,128)}), f32[4,8,512]{2,1,0:T(8,128)S(1)}, u32[]{:S(2)}, u32[]{:S(2)}) async-start(f32[4,8,512]{2,1,0:T(8,128)} %tile.2), calls=%async_computation.1 | async-start | bytes 131072 | tf_op jit(solution)/shard_map/all_to_all | solution.py:136
  74.3 4.5 %collective-permute-start.4 = (f32[4,512]{1,0:T(4,128)S(1)}, f32[4,512]{1,0:T(4,128)S(1)}, u32[]{:S(2)}, u32[]{:S(2)}) collective-permute-start(f32[4,512]{1,0:T(4,128)S(1)} %get-tuple-element.134), channel_id=1, source_target_pairs={{2,0},{4,2},{6,4},{3,1},{5,3},{7,5},{10,8},{12,10},{14,12},{11,9},... | collective-permute-start | bytes 24584 | tf_op jit(solution)/shard_map/ppermute | solution.py:22
  75.6 3.8 %collective-permute-start.3 = (f32[4,512]{1,0:T(4,128)S(1)}, f32[4,512]{1,0:T(4,128)S(1)}, u32[]{:S(2)}, u32[]{:S(2)}) collective-permute-start(f32[4,512]{1,0:T(4,128)S(1)} %get-tuple-element.133), channel_id=1, source_target_pairs={{0,2},{2,4},{4,6},{1,3},{3,5},{5,7},{8,10},{10,12},{12,14},{9,11},... | collective-permute-start | bytes 24584 | tf_op jit(solution)/shard_map/ppermute | solution.py:21
  79.5 4.0 %collective-permute-start.5 = (f32[4,40]{0,1:T(8,128)S(1)}, f32[4,40]{0,1:T(8,128)S(1)}, u32[]{:S(2)}, u32[]{:S(2)}) collective-permute-start(f32[4,40]{0,1:T(8,128)S(1)} %fusion.56), channel_id=1, source_target_pairs={{0,1},{1,0},{2,3},{3,2},{4,5},{5,4},{6,7},{7,6},{8,9},{9,8},{10,11... | collective-permute-start | bytes 1928 | tf_op jit(solution)/shard_map/ppermute | solution.py:41
